TPU v7x, 128 devices: a whole 4x4x4 slice. The times are simulated.
128 devices in a mesh: outer: 4 (over z), inner: 32 (over y, x, core).
Axes of the slice: x: 4, y: 4, z: 4, core: 2. Of those that a mesh axis runs over, the one named last changes fastest.
Arguments:
- tiles: bfloat16 [65536, 128, 128], P(('outer', 'inner')), as said below
- tile_row: int32 [65536], P(('outer', 'inner')), may hold values from 0 to 3, as said below
- tile_col: int32 [65536], P(('outer', 'inner')), may hold values from 0 to 3, as said below
- counts: int32 [16384], P(('outer', 'inner')), may hold values from 1 to 4, as said below
- vectors: bfloat16 [65536, 64], P(('outer', 'inner')), may hold values from -6 to 6
Outputs:
- basis: float32 [65536, 64], P(('outer', 'inner'))
- degree: float32 [65536], P(('outer', 'inner'))
Inputs may be any that keep to these rules, and one draw needn't show every extreme that they name: Slot s from sender g to destination h is live exactly when s < counts[g * 128 + h]; the tiles of dead slots hold values that are no part of P. counts is 4 from every sender to itself and 1 to 4 from every sender to every other destination. `tile_row`: A slot from a sender to itself with number s lies in block row s % 4. `tile_col`: A slot from a sender to itself with number s lies in block column s % 4. `tiles`: entries are affinities, zero or positive.
All inputs are finite; a program needn't handle non-finite values.
Results may differ from a plain program's by a relative error of at most 0.004.
Values may be sent and summed in bfloat16 or wider, within the bound.
No kernel may reach another device: no remote copies, remote signals or barrier semaphores. Data moves between devices by JAX's collectives and lax.ppermute only.
A program may use at most 192 MiB of HBM per device.

v0:
```python
import jax
import jax.numpy as jnp
from jax import lax
from jax.sharding import PartitionSpec as P


def shards(tiles, tile_row, tile_col, counts, vectors):
    peer_count = lax.axis_size(("outer", "inner"))
    slot_count = tiles.shape[0] // peer_count
    tile_size = tiles.shape[1]
    rows_dev = vectors.shape[0]
    block_count = rows_dev // tile_size
    vec_width = vectors.shape[1]
    highest = lax.Precision.HIGHEST
    got_tiles, got_rows, got_cols, got_counts = (
        lax.all_to_all(tiles, ("outer", "inner"), split_axis=0, concat_axis=0, tiled=True),
        lax.all_to_all(tile_row, ("outer", "inner"), split_axis=0, concat_axis=0, tiled=True),
        lax.all_to_all(tile_col, ("outer", "inner"), split_axis=0, concat_axis=0, tiled=True),
        lax.all_to_all(counts, ("outer", "inner"), split_axis=0, concat_axis=0, tiled=True),
    )
    got_sums = jnp.sum(got_tiles, axis=1, dtype=jnp.float32)
    slot_number = jnp.arange(slot_count, dtype=jnp.int32)[None, :]
    own_live = (slot_number < counts[:, None]).reshape(-1).astype(jnp.float32)
    got_live = (slot_number < got_counts[:, None]).reshape(-1).astype(jnp.float32)
    block_ids = jnp.arange(block_count, dtype=jnp.int32)[None, :]
    own_weight = (tile_row[:, None] == block_ids).astype(jnp.float32) * own_live[:, None]
    got_weight = (got_cols[:, None] == block_ids).astype(jnp.float32) * got_live[:, None]
    own_sums = jnp.sum(tiles, axis=2, dtype=jnp.float32)
    degree_blocks = jnp.einsum("tr,ta->ra", own_weight, own_sums, precision=highest)
    degree_blocks = degree_blocks + jnp.einsum("tr,ta->ra", got_weight, got_sums, precision=highest)
    degree = 1.0 + degree_blocks.reshape(rows_dev)
    inv_root = lax.rsqrt(degree)
    scaled = (inv_root[:, None] * vectors.astype(jnp.float32)).astype(jnp.bfloat16)

    def piece_layout(piece, start):
        piece_devs = piece.shape[0] // rows_dev
        first_dev = start // rows_dev
        block_vec = piece.reshape(piece_devs, block_count, tile_size, vec_width)
        source_idx = jnp.repeat(jnp.arange(piece_devs, dtype=jnp.int32), slot_count)
        return (block_vec, source_idx, first_dev * slot_count, piece_devs * slot_count)

    empty = jnp.zeros((block_count, tile_size, vec_width), jnp.float32)
    group_vec = lax.all_gather(scaled, "inner", axis=0, tiled=True)
    piece = lax.all_gather(group_vec, "outer", axis=0, tiled=True)
    start = jnp.int32(0)
    block_vec, source_idx, begin, length = piece_layout(piece, start)
    forward = jnp.einsum(
        "tab,tbk->tak", tiles, block_vec[source_idx, tile_col], preferred_element_type=jnp.float32
    )
    block_vec, source_idx, begin, length = piece_layout(piece, start)
    got_mix = got_weight.astype(jnp.bfloat16)
    mirrored = jnp.einsum(
        "tba,tbk->tak",
        got_tiles,
        block_vec[source_idx, got_rows],
        preferred_element_type=jnp.float32,
    )
    total = jnp.einsum("tr,tak->rak", own_weight, forward, precision=highest) + jnp.einsum(
        "tr,tak->rak", got_mix, mirrored.astype(jnp.bfloat16), preferred_element_type=jnp.float32
    )
    total = total + empty
    image = inv_root[:, None] * (total.reshape(rows_dev, vec_width) + scaled.astype(jnp.float32))
    local_gram = jnp.dot(image.T, image, precision=highest)
    gram = lax.psum(local_gram, ("outer", "inner")) / jnp.float32(rows_dev * peer_count)
    lower = jnp.linalg.cholesky(gram)
    basis = jax.scipy.linalg.solve_triangular(lower, image.T, lower=True).T
    return (basis, degree)


def solution(mesh):
    placed = (
        P(("outer", "inner"), None, None),
        P(("outer", "inner")),
        P(("outer", "inner")),
        P(("outer", "inner")),
        P(("outer", "inner"), None),
    )
    return jax.shard_map(
        shards,
        mesh=mesh,
        in_specs=placed,
        out_specs=(P(("outer", "inner"), None), P(("outer", "inner"))),
        check_vma=False,
    )
```

profile of v0, /device:TPU:1, one launch (start us, length us, event | category | flops | bytes accessed | tf_op | source)
XLA Modules:
  0.0 626.3 jit_solution(13226330766518004586)
XLA Ops:
  7.2 1.4 copy.27
  8.6 11.5 %all-to-all-start.1 = ((s32[128,1,1]{2,1,0:T(1,128)}), s32[128,1,1]{2,1,0:T(1,128)S(1)}, u32[]{:S(2)}, u32[]{:S(2)}) async-start(s32[128,1,1]{2,1,0:T(1,128)} %copy.27), calls=%async_computation.1 | async-start | bytes 131072 | tf_op jit(solution)/shard_map/all_to_all | solution.py:19
  20.1 0.8 all_to_all.23
  20.9 8.7 %all-to-all-done.1 = s32[128,1,1]{2,1,0:T(1,128)S(1)} async-done(((s32[128,1,1]{2,1,0:T(1,128)}), s32[128,1,1]{2,1,0:T(1,128)S(1)}, u32[]{:S(2)}, u32[]{:S(2)}) %all-to-all-start.1) | async-done | bytes 544 | tf_op jit(solution)/shard_map/all_to_all | solution.py:19
  29.6 13.9 %all_to_all.35 = s32[128,4,1]{1,2,0:T(1,128)S(1)} all-to-all(s32[128,4,1]{1,2,0:T(1,128)S(1)} %bitcast.50), channel_id=1, replica_groups=mesh['outer'=4,'inner'=32] {'outer','inner'}, dimensions={0} | all-to-all | bytes 4096 | tf_op jit(solution)/shard_map/all_to_all | solution.py:18
  43.5 5.6 all-to-all-start.2
  49.4 10.0 %convert_reduce_fusion.1 = f32[512,128]{1,0:T(8,128)S(1)} fusion(bf16[512,128,128]{2,1,0:T(8,128)(2,1)} %param.5), kind=kLoop, calls=%fused_computation.3 | loop fusion | flops 16711680 | bytes 17039360 | tf_op jit(solution)/shard_map/reduce_sum | solution.py:28
  59.7 2.4 reduce.7
  62.7 0.7 reduce.13
  63.5 197.5 %all-to-all-done.2 = bf16[512,128,128]{2,1,0:T(8,128)(2,1)} async-done(((bf16[512,128,128]{2,1,0:T(8,128)(2,1)}), bf16[512,128,128]{2,1,0:T(8,128)(2,1)}, u32[]{:S(2)}, u32[]{:S(2)}) %all-to-all-start.2) | async-done | bytes 16777248 | tf_op jit(solution)/shard_map/all_to_all | solution.py:16
  261.1 6.9 %convert_reduce_fusion = f32[512,128]{1,0:T(8,128)S(1)} fusion(bf16[512,128,128]{2,1,0:T(8,128)(2,1)} %all-to-all-done.2), kind=kLoop, calls=%fused_computation.2 | loop fusion | flops 16711680 | bytes 17039360 | tf_op jit(solution)/shard_map/reduce_sum | solution.py:21
  267.9 0.8 fusion.50
  269.5 75.4 %all-gather.3.cloned.1.call-done = bf16[16384,64]{0,1:T(8,128)(2,1)} async-done(((bf16[512,64]{0,1:T(8,128)(2,1)}), bf16[16384,64]{0,1:T(8,128)(2,1)}) %all-gather.3.cloned.1.call-update) | async-done | bytes 2097168 | tf_op jit(solution)/shard_map/all_gather | solution.py:43
  344.9 0.7 all_to_all.28
  345.7 7.9 %all-to-all-start.3 = ((s32[128,4,1]{1,2,0:T(1,128)}), s32[128,4,1]{1,2,0:T(1,128)S(1)}, u32[]{:S(2)}, u32[]{:S(2)}) async-start(s32[128,4,1]{1,2,0:T(1,128)} %bitcast.8), calls=%async_computation.3 | async-start | bytes 131072 | tf_op jit(solution)/shard_map/all_to_all | solution.py:17
  353.7 9.4 %all-to-all-done.3 = s32[128,4,1]{1,2,0:T(1,128)S(1)} async-done(((s32[128,4,1]{1,2,0:T(1,128)}), s32[128,4,1]{1,2,0:T(1,128)S(1)}, u32[]{:S(2)}, u32[]{:S(2)}) %all-to-all-start.3) | async-done | bytes 2080 | tf_op jit(solution)/shard_map/all_to_all | solution.py:17
  363.1 0.7 reduce.14
  364.0 65.3 %all-gather.5.cloned.1.call-done = bf16[65536,64]{0,1:T(8,128)(2,1)} async-done(((bf16[16384,64]{0,1:T(8,128)(2,1)}), bf16[65536,64]{0,1:T(8,128)(2,1)}) %all-gather.5.cloned.1.call-update) | async-done | bytes 8388624 | tf_op jit(solution)/shard_map/all_gather | solution.py:44
  429.2 11.8 %reshape.136 = bf16[128,4,128,64]{2,1,0,3:T(4,128)(2,1)} reshape(bf16[65536,64]{0,1:T(8,128)(2,1)} %all-gather.5.cloned.1.call-done) | data formatting | bytes 16777216 | tf_op jit(solution)/shard_map/reshape | solution.py:38
  441.0 16.3 %copy.28 = bf16[128,4,128,64]{2,3,1,0:T(8,128)(2,1)} copy(bf16[128,4,128,64]{2,1,0,3:T(4,128)(2,1)} %reshape.136) | data formatting | bytes 16777216 | tf_op jit(solution)/shard_map/reshape | solution.py:38
  457.3 11.1 %gather_fusion.1 = bf16[512,128,64]{1,2,0:T(8,128)(2,1)} fusion(bf16[128,4,128,64]{2,3,1,0:T(8,128)(2,1)} %copy.28, s32[512]{0:T(512)S(1)} %bitcast.47), kind=kCustom, calls=%fused_computation.1 | custom fusion | bytes 16781312 | tf_op jit(solution)/shard_map/gather | solution.py:55
  468.5 11.0 %gather_fusion = bf16[512,128,64]{1,2,0:T(8,128)(2,1)} fusion(bf16[128,4,128,64]{2,3,1,0:T(8,128)(2,1)} %copy.28, s32[512]{0:T(512)S(1)} %bitcast.46), kind=kCustom, calls=%fused_computation | custom fusion | bytes 16781312 | tf_op jit(solution)/shard_map/gather | solution.py:48
  479.4 19.6 %convolution_bitcast_fusion = f32[512,128,64]{1,2,0:T(8,128)} fusion(bf16[512,128,64]{1,2,0:T(8,128)(2,1)} %gather_fusion, bf16[512,128,128]{2,1,0:T(8,128)(2,1)} %param.5), kind=kOutput, calls=%fused_computation.6 | convolution fusion | flops 1073741824 | bytes 41943040 | tf_op jit(solution)/shard_map/tab,tbk->tak/dot_general | solution.py:47
  499.0 23.4 %fusion = f32[4,128,64]{1,0,2:T(4,128)S(1)} fusion(f32[512,128,64]{1,2,0:T(8,128)} %convolution_bitcast_fusion, f32[512]{0:T(512)S(1)} %reshape.139, s32[512]{0:T(512)S(1)} %copy-done.2), kind=kOutput, calls=%fused_computation.4 | convolution fusion | flops 201330688 | bytes 16912384 | tf_op jit(solution)/shard_map/tr,tak->rak/dot_general | solution.py:58
  522.4 10.5 %convert_bitcast_fusion = bf16[512,128,64]{1,2,0:T(8,128)(2,1)} fusion(bf16[512,128,64]{1,2,0:T(8,128)(2,1)S(1)} %copy-done, bf16[512,128,128]{2,1,0:T(8,128)(2,1)} %all-to-all-done.2), kind=kOutput, calls=%fused_computation.9 | convolution fusion | flops 1077936128 | bytes 33554432 | tf_op jit(solution)/shard_map/tba,tbk->tak/dot_general | solution.py:52
  532.9 7.9 %fusion.4 = f32[4,128,64]{1,0,2:T(4,128)S(1)} fusion(f32[4,128,64]{1,0,2:T(4,128)S(1)} %fusion, bf16[512,128,64]{1,2,0:T(8,128)(2,1)} %convert_bitcast_fusion, f32[512]{0:T(512)S(1)} %reshape.140, s32[512]{0:T(512)S(1)} %eq.31), kind=kOutput, calls=%fused_computation.10 | convolution fusion | flops 33591296 | bytes 8654848 | tf_op jit(solution)/shard_map/tr,tak->rak/dot_general | solution.py:58
  541.1 65.0 %psum.7 = f32[64,64]{0,1:T(8,128)S(1)} all-reduce(f32[64,64]{0,1:T(8,128)S(1)} %fusion.12), channel_id=1, replica_groups=mesh['outer'=4,'inner'=32] {'outer','inner'}, use_global_device_ids=true, to_apply=%region_2.0 | all-reduce | flops 4096 | bytes 32768 | tf_op jit(solution)/shard_map/psum | solution.py:64
  606.2 5.8 cholesky.16
  612.0 0.6 compare_reduce_fusion
  612.7 0.7 fusion.18
  613.3 4.9 custom-call.7
  618.2 1.0 fusion.10
  (32 shorter events, 2.6 us)
Async XLA Ops:
  8.6 21.0 %all-to-all-start.1 = ((s32[128,1,1]{2,1,0:T(1,128)}), s32[128,1,1]{2,1,0:T(1,128)S(1)}, u32[]{:S(2)}, u32[]{:S(2)}) async-start(s32[128,1,1]{2,1,0:T(1,128)} %copy.27), calls=%async_computation.1 | async-start | bytes 131072 | tf_op jit(solution)/shard_map/all_to_all | solution.py:19
  43.5 5.7 copy-start.4
  43.5 217.6 %all-to-all-start.2 = ((bf16[512,128,128]{2,1,0:T(8,128)(2,1)}), bf16[512,128,128]{2,1,0:T(8,128)(2,1)}, u32[]{:S(2)}, u32[]{:S(2)}) async-start(bf16[512,128,128]{2,1,0:T(8,128)(2,1)} %param.5), calls=%async_computation.2 | async-start | bytes 33554432 | tf_op jit(solution)/shard_map/all_to_all | solution.py:16
  49.1 10.3 %copy-start.2 = (s32[512]{0:T(512)S(1)}, s32[512]{0:T(512)}, u32[]{:S(2)}) copy-start(s32[512]{0:T(512)} %param.6) | copy-start | bytes 6148
  49.1 295.8 %all-gather.3.cloned.1.call-start = ((), (), s32[]{:S(2)}) async-start(), calls=%async_computation.4 | async-start | bytes 2162688 | tf_op jit(solution)/shard_map/all_gather | solution.py:43
  49.4 219.4 %copy-start.1 = (bf16[512,64]{0,1:T(8,128)(2,1)S(1)}, bf16[512,64]{0,1:T(8,128)(2,1)}, u32[]{:S(2)}) copy-start(bf16[512,64]{0,1:T(8,128)(2,1)} %param.9) | copy-start | bytes 196612
  49.4 304.2 %copy-start.3 = (s32[512]{0:T(512)S(1)}, s32[512]{0:T(512)}, u32[]{:S(2)}) copy-start(s32[512]{0:T(512)} %param.7) | copy-start | bytes 6148
  269.5 159.8 %all-gather.5.cloned.1.call-start = ((), (), s32[]{:S(2)}) async-start(), calls=%async_computation.5 | async-start | bytes 10485760 | tf_op jit(solution)/shard_map/all_gather | solution.py:44
  345.7 17.5 %all-to-all-start.3 = ((s32[128,4,1]{1,2,0:T(1,128)}), s32[128,4,1]{1,2,0:T(1,128)S(1)}, u32[]{:S(2)}, u32[]{:S(2)}) async-start(s32[128,4,1]{1,2,0:T(1,128)} %bitcast.8), calls=%async_computation.3 | async-start | bytes 131072 | tf_op jit(solution)/shard_map/all_to_all | solution.py:17
  499.0 23.4 %copy-start = (bf16[512,128,64]{1,2,0:T(8,128)(2,1)S(1)}, bf16[512,128,64]{1,2,0:T(8,128)(2,1)}, u32[]{:S(2)}) copy-start(bf16[512,128,64]{1,2,0:T(8,128)(2,1)} %gather_fusion.1) | copy-start | bytes 25165828
Sparse Core Ops, SparseCore 0:
  269.6 75.2 all-gather.2
  346.6 82.6 all-gather.4
where the time goes:
time: 632 us; the launch traced here: 626 us
  waiting for transfers between devices  356 us (56%)
  blocking collectives  78.9 us (12%)
  matrix products  63.7 us (10%)
  local copies, waits for them, and re-layouts  54.2 us (9%)
  other arithmetic  33.5 us (5%)
  starting transfers between devices  25.1 us (4%)
  between operations  14.5 us (2%)
    all_to_all x1, waiting for transfers between devices, shards(): lax.all_to_all(tiles, ('outer', 'inner'), split_axis=0, concat_axis=0, ti...  198 us
    all_gather x1, waiting for transfers between devices, shards(): group_vec = lax.all_gather(scaled, 'inner', axis=0, tiled=True)  75.4 us
    all_gather x1, waiting for transfers between devices, shards(): piece = lax.all_gather(group_vec, 'outer', axis=0, tiled=True)  65.3 us
    psum x1, blocking collectives, shards(): lax.psum(local_gram, ('outer', 'inner'))  65 us
    reshape x2, local copies, waits for them, and re-layouts, piece_layout(): block_vec = piece.reshape(piece_devs, block_count, tile_size, vec_width)  28.1 us
    dot_general x1, matrix products, shards(): jnp.einsum('tr,tak->rak', own_weight, forward, precision=highest)  23.4 us
    dot_general x1, matrix products, shards(): jnp.einsum('tab,tbk->tak', tiles, block_vec[source_idx, tile_col], prefer...  19.6 us
    all_to_all x1, blocking collectives, shards(): lax.all_to_all(tile_col, ('outer', 'inner'), split_axis=0, concat_axis=0,...  13.9 us
  transfers between devices with their start and end apart: 5, of which 5 were waited for; matrix products, arithmetic and copies ran while one was open for 2% of the time, Pallas kernels for 0%

commit v1 on v0

--- a/solution.py
+++ b/solution.py
@@ -1,7 +1,40 @@
+import functools
 import jax
 import jax.numpy as jnp
 from jax import lax
 from jax.sharding import PartitionSpec as P
+from jax.lax import axis_index, axis_size, ppermute
+
+
+def check_layers_all(mine, array_dim):
+    moved = list(mine.shape[1:])
+    moved[array_dim] *= mine.shape[0]
+    return jnp.moveaxis(mine, 0, array_dim).reshape(moved)
+
+
+def copies_pair(obj, axis_tag, along_dim):
+    dev_count = axis_size(axis_tag)
+    line_up = []
+    for tick in range(dev_count):
+        line_up.append((tick, (tick + 1) % dev_count))
+    blocks_here = []
+    for p, kk in line_up:
+        blocks_here.append((kk, p))
+    mid_arr, seen_now = ([], [])
+    for ix in range(dev_count - 1):
+        if ix % 2 == 0:
+            raw_out = ppermute(mid_arr[-1] if mid_arr else obj, axis_tag, line_up)
+            mid_arr.append(raw_out)
+        else:
+            seen_now.append(ppermute(seen_now[-1] if seen_now else obj, axis_tag, blocks_here))
+    x_next = jnp.stack([*mid_arr[::-1], obj, *seen_now])
+    answer = axis_index(axis_tag)
+    local_part = answer - len(mid_arr)
+    x_next = x_next[(jnp.arange(dev_count) - local_part) % dev_count]
+    return check_layers_all(x_next, along_dim)
+
+
+place_spot = functools.partial(copies_pair, axis_tag="outer", along_dim=0)
 
 
 def shards(tiles, tile_row, tile_col, counts, vectors):
@@ -41,7 +74,7 @@
 
     empty = jnp.zeros((block_count, tile_size, vec_width), jnp.float32)
     group_vec = lax.all_gather(scaled, "inner", axis=0, tiled=True)
-    piece = lax.all_gather(group_vec, "outer", axis=0, tiled=True)
+    piece = place_spot(group_vec)
     start = jnp.int32(0)
     block_vec, source_idx, begin, length = piece_layout(piece, start)
     forward = jnp.einsum(

time: 632 us -> 691 us (1.093)
  local copies, waits for them, and re-layouts: 54.2 us -> 83.9 us
  waiting for transfers between devices: 356 us -> 368 us
  other arithmetic: 33.5 us -> 45.2 us
    all_gather x1 -> x0, waiting for transfers between devices: 65.3 us -> none  [shards(): piece = lax.all_gather(group_vec, 'outer', axis=0, tiled=True)]
    ppermute x0 -> x3, waiting for transfers between devices: none -> 45.7 us  [the longest x2 45.7 us: copies_pair(): raw_out = ppermute(mid_arr[-1] if mid_arr else obj, axis_tag, line_up)]
    another operation x0 -> x2, local copies, waits for them, and re-layouts: none -> 32.2 us  [piece_layout(): block_vec = piece.reshape(piece_devs, block_count, tile_size, vec_width)]
    all_to_all x1, waiting for transfers between devices: 9.39 us -> 40.5 us  [shards(): lax.all_to_all(tile_row, ('outer', 'inner'), split_axis=0, concat_axis=0,...]
    reshape x2 -> x0, local copies, waits for them, and re-layouts: 28.1 us -> none  [piece_layout(): block_vec = piece.reshape(piece_devs, block_count, tile_size, vec_width)]
    gather x0 -> x3, local copies, waits for them, and re-layouts: none -> 13.6 us  [copies_pair(): x_next = x_next[(jnp.arange(dev_count) - local_part) % dev_count]]
    unnamed x10 -> x11, local copies, waits for them, and re-layouts: 0.03 us -> 12.1 us
    unnamed x0 -> x1, other arithmetic: none -> 7.56 us
  transfers between devices with their start and end apart: 5 -> 7, of which waited for: 5 -> 5; matrix products, arithmetic and copies ran while one was open for 2% -> 2% of each run, Pallas kernels for 0% -> 0%
where the time goes in v1:
time: 691 us; the launch traced here: 681 us
  waiting for transfers between devices  368 us (53%)
  local copies, waits for them, and re-layouts  83.9 us (12%)
  blocking collectives  77.8 us (11%)
  matrix products  63.9 us (9%)
  other arithmetic  45.2 us (7%)
  starting transfers between devices  28.1 us (4%)
  between operations  14.7 us (2%)
    all_to_all x1, waiting for transfers between devices, shards(): lax.all_to_all(tiles, ('outer', 'inner'), split_axis=0, concat_axis=0, ti...  197 us
    all_gather x1, waiting for transfers between devices, shards(): group_vec = lax.all_gather(scaled, 'inner', axis=0, tiled=True)  75.4 us
    psum x1, blocking collectives, shards(): lax.psum(local_gram, ('outer', 'inner'))  63.9 us
    ppermute x2, waiting for transfers between devices, copies_pair(): raw_out = ppermute(mid_arr[-1] if mid_arr else obj, axis_tag, line_up)  45.7 us
    all_to_all x1, waiting for transfers between devices, shards(): lax.all_to_all(tile_row, ('outer', 'inner'), split_axis=0, concat_axis=0,...  40.5 us
    another operation x2, local copies, waits for them, and re-layouts, piece_layout(): block_vec = piece.reshape(piece_devs, block_count, tile_size, vec_width)  32.2 us
    dot_general x1, matrix products, shards(): jnp.einsum('tr,tak->rak', own_weight, forward, precision=highest)  23.4 us
    dot_general x1, matrix products, shards(): jnp.einsum('tab,tbk->tak', tiles, block_vec[source_idx, tile_col], prefer...  19.8 us
  transfers between devices with their start and end apart: 7, of which 5 were waited for; matrix products, arithmetic and copies ran while one was open for 2% of the time, Pallas kernels for 0%

profile of v1, /device:TPU:1, one launch (start us, length us, event | category | flops | bytes accessed | tf_op | source)
XLA Modules:
  0.0 681.3 jit_solution(9434936243840432665)
XLA Ops:
  7.2 1.4 copy.30
  8.6 11.5 %all-to-all-start.1 = ((s32[128,1,1]{2,1,0:T(1,128)}), s32[128,1,1]{2,1,0:T(1,128)S(1)}, u32[]{:S(2)}, u32[]{:S(2)}) async-start(s32[128,1,1]{2,1,0:T(1,128)} %copy.30), calls=%async_computation.1 | async-start | bytes 131072 | tf_op jit(solution)/shard_map/all_to_all | solution.py:52
  20.9 8.7 %all-to-all-done.1 = s32[128,1,1]{2,1,0:T(1,128)S(1)} async-done(((s32[128,1,1]{2,1,0:T(1,128)}), s32[128,1,1]{2,1,0:T(1,128)S(1)}, u32[]{:S(2)}, u32[]{:S(2)}) %all-to-all-start.1) | async-done | bytes 544 | tf_op jit(solution)/shard_map/all_to_all | solution.py:52
  29.6 13.9 %all_to_all.35 = s32[128,4,1]{1,2,0:T(1,128)S(1)} all-to-all(s32[128,4,1]{1,2,0:T(1,128)S(1)} %bitcast.58), channel_id=1, replica_groups=mesh['outer'=4,'inner'=32] {'outer','inner'}, dimensions={0} | all-to-all | bytes 4096 | tf_op jit(solution)/shard_map/all_to_all | solution.py:51
  43.5 5.6 all-to-all-start.2
  49.4 10.0 %convert_reduce_fusion.1 = f32[512,128]{1,0:T(8,128)S(1)} fusion(bf16[512,128,128]{2,1,0:T(8,128)(2,1)} %param.5), kind=kLoop, calls=%fused_computation.5 | loop fusion | flops 16711680 | bytes 17039360 | tf_op jit(solution)/shard_map/reduce_sum | solution.py:61
  59.6 2.4 reduce.7
  63.7 197.4 %all-to-all-done.2 = bf16[512,128,128]{2,1,0:T(8,128)(2,1)} async-done(((bf16[512,128,128]{2,1,0:T(8,128)(2,1)}), bf16[512,128,128]{2,1,0:T(8,128)(2,1)}, u32[]{:S(2)}, u32[]{:S(2)}) %all-to-all-start.2) | async-done | bytes 16777248 | tf_op jit(solution)/shard_map/all_to_all | solution.py:49
  261.1 6.9 %convert_reduce_fusion = f32[512,128]{1,0:T(8,128)S(1)} fusion(bf16[512,128,128]{2,1,0:T(8,128)(2,1)} %all-to-all-done.2), kind=kLoop, calls=%fused_computation.4 | loop fusion | flops 16711680 | bytes 17039360 | tf_op jit(solution)/shard_map/reduce_sum | solution.py:54
  269.5 75.4 %all-gather.2.cloned.1.call-done = bf16[16384,64]{0,1:T(8,128)(2,1)} async-done(((bf16[512,64]{0,1:T(8,128)(2,1)}), bf16[16384,64]{0,1:T(8,128)(2,1)}) %all-gather.2.cloned.1.call-update) | async-done | bytes 2097168 | tf_op jit(solution)/shard_map/all_gather | solution.py:76
  344.9 1.3 collective-permute-start
  346.2 1.4 collective-permute-start.2
  347.6 45.7 %collective-permute-done = bf16[16384,64]{0,1:T(8,128)(2,1)S(1)} collective-permute-done((bf16[16384,64]{0,1:T(8,128)(2,1)}, bf16[16384,64]{0,1:T(8,128)(2,1)S(1)}, u32[]{:S(2)}, u32[]{:S(2)}) %collective-permute-start) | collective-permute-done | bytes 2097184 | tf_op jit(solution)/shard_map/ppermute | solution.py:26
  394.2 8.1 %all-to-all-start.3 = ((s32[128,4,1]{1,2,0:T(1,128)}), s32[128,4,1]{1,2,0:T(1,128)S(1)}, u32[]{:S(2)}, u32[]{:S(2)}) async-start(s32[128,4,1]{1,2,0:T(1,128)} %bitcast.13), calls=%async_computation.3 | async-start | bytes 131072 | tf_op jit(solution)/shard_map/all_to_all | solution.py:50
  402.5 40.5 %all-to-all-done.3 = s32[128,4,1]{1,2,0:T(1,128)S(1)} async-done(((s32[128,4,1]{1,2,0:T(1,128)}), s32[128,4,1]{1,2,0:T(1,128)S(1)}, u32[]{:S(2)}, u32[]{:S(2)}) %all-to-all-start.3) | async-done | bytes 2080 | tf_op jit(solution)/shard_map/all_to_all | solution.py:50
  443.9 3.8 pad_maximum_fusion
  447.7 3.6 fusion.52
  451.4 5.0 gather_fusion.2
  456.4 4.9 gather_fusion.3
  461.3 7.6 %pad_maximum_fusion.1 = bf16[4,16384,64]{1,2,0:T(8,128)(2,1)} fusion(bf16[4,8192,64]{1,2,0:T(8,128)(2,1)} %gather_fusion.3, bf16[4,8192,64]{1,2,0:T(8,128)(2,1)} %gather_fusion.2), kind=kLoop, calls=%fused_computation.10 | loop fusion | flops 16777216 | bytes 16777216
  468.9 12.1 %copy.31 = bf16[4,16384,64]{1,0,2:T(4,128)(2,1)} copy(bf16[4,16384,64]{1,2,0:T(8,128)(2,1)} %pad_maximum_fusion.1) | data formatting | bytes 16777216
  481.0 15.9 %reshape_reshape.4 = bf16[128,4,128,64]{2,1,0,3:T(4,128)(2,1)} reshape(bf16[4,16384,64]{1,0,2:T(4,128)(2,1)} %copy.31) | data formatting | bytes 16777216 | tf_op jit(solution)/shard_map/reshape;reshape | solution.py:71
  496.8 16.3 %copy.32 = bf16[128,4,128,64]{2,3,1,0:T(8,128)(2,1)} copy(bf16[128,4,128,64]{2,1,0,3:T(4,128)(2,1)} %reshape_reshape.4) | data formatting | bytes 16777216 | tf_op jit(solution)/shard_map/reshape;reshape | solution.py:71
  513.2 11.0 %gather_fusion.1 = bf16[512,128,64]{1,2,0:T(8,128)(2,1)} fusion(bf16[128,4,128,64]{2,3,1,0:T(8,128)(2,1)} %copy.32, s32[512]{0:T(512)S(1)} %bitcast.53), kind=kCustom, calls=%fused_computation.1 | custom fusion | bytes 16781312 | tf_op jit(solution)/shard_map/gather | solution.py:88
  524.1 11.0 %gather_fusion = bf16[512,128,64]{1,2,0:T(8,128)(2,1)} fusion(bf16[128,4,128,64]{2,3,1,0:T(8,128)(2,1)} %copy.32, s32[512]{0:T(512)S(1)} %bitcast.52), kind=kCustom, calls=%fused_computation | custom fusion | bytes 16781312 | tf_op jit(solution)/shard_map/gather | solution.py:81
  535.1 19.8 %convolution_bitcast_fusion = f32[512,128,64]{1,2,0:T(8,128)} fusion(bf16[512,128,64]{1,2,0:T(8,128)(2,1)} %gather_fusion, bf16[512,128,128]{2,1,0:T(8,128)(2,1)} %param.5), kind=kOutput, calls=%fused_computation.8 | convolution fusion | flops 1073741824 | bytes 41943040 | tf_op jit(solution)/shard_map/tab,tbk->tak/dot_general | solution.py:80
  554.9 23.4 %fusion = f32[4,128,64]{1,0,2:T(4,128)S(1)} fusion(f32[512,128,64]{1,2,0:T(8,128)} %convolution_bitcast_fusion, f32[512]{0:T(512)S(1)} %reshape.183, s32[512]{0:T(512)S(1)} %copy-done.2), kind=kOutput, calls=%fused_computation.6 | convolution fusion | flops 201330688 | bytes 16912384 | tf_op jit(solution)/shard_map/tr,tak->rak/dot_general | solution.py:91
  578.2 10.6 %convert_bitcast_fusion = bf16[512,128,64]{1,2,0:T(8,128)(2,1)} fusion(bf16[512,128,64]{1,2,0:T(8,128)(2,1)S(1)} %copy-done, bf16[512,128,128]{2,1,0:T(8,128)(2,1)} %all-to-all-done.2), kind=kOutput, calls=%fused_computation.13 | convolution fusion | flops 1077936128 | bytes 33554432 | tf_op jit(solution)/shard_map/tba,tbk->tak/dot_general | solution.py:85
  588.8 7.9 %fusion.4 = f32[4,128,64]{1,0,2:T(4,128)S(1)} fusion(f32[4,128,64]{1,0,2:T(4,128)S(1)} %fusion, bf16[512,128,64]{1,2,0:T(8,128)(2,1)} %convert_bitcast_fusion, f32[512]{0:T(512)S(1)} %reshape.184, s32[512]{0:T(512)S(1)} %eq.33), kind=kOutput, calls=%fused_computation.14 | convolution fusion | flops 33591296 | bytes 8654848 | tf_op jit(solution)/shard_map/tr,tak->rak/dot_general | solution.py:91
  596.9 63.9 %psum.7 = f32[64,64]{0,1:T(8,128)S(1)} all-reduce(f32[64,64]{0,1:T(8,128)S(1)} %fusion.12), channel_id=1, replica_groups=mesh['outer'=4,'inner'=32] {'outer','inner'}, use_global_device_ids=true, to_apply=%region_2.3 | all-reduce | flops 4096 | bytes 32768 | tf_op jit(solution)/shard_map/psum | solution.py:97
  660.9 5.8 cholesky.16
  668.1 4.9 custom-call.7
  (43 shorter events, 9.1 us)
Async XLA Ops:
  8.6 21.0 %all-to-all-start.1 = ((s32[128,1,1]{2,1,0:T(1,128)}), s32[128,1,1]{2,1,0:T(1,128)S(1)}, u32[]{:S(2)}, u32[]{:S(2)}) async-start(s32[128,1,1]{2,1,0:T(1,128)} %copy.30), calls=%async_computation.1 | async-start | bytes 131072 | tf_op jit(solution)/shard_map/all_to_all | solution.py:52
  43.5 5.7 copy-start.4
  43.5 217.6 %all-to-all-start.2 = ((bf16[512,128,128]{2,1,0:T(8,128)(2,1)}), bf16[512,128,128]{2,1,0:T(8,128)(2,1)}, u32[]{:S(2)}, u32[]{:S(2)}) async-start(bf16[512,128,128]{2,1,0:T(8,128)(2,1)} %param.5), calls=%async_computation.2 | async-start | bytes 33554432 | tf_op jit(solution)/shard_map/all_to_all | solution.py:49
  49.1 295.8 %all-gather.2.cloned.1.call-start = ((), (), s32[]{:S(2)}) async-start(), calls=%async_computation.4 | async-start | bytes 2162688 | tf_op jit(solution)/shard_map/all_gather | solution.py:76
  49.4 10.0 %copy-start.2 = (s32[512]{0:T(512)S(1)}, s32[512]{0:T(512)}, u32[]{:S(2)}) copy-start(s32[512]{0:T(512)} %param.6) | copy-start | bytes 6148
  63.7 205.1 %copy-start.1 = (bf16[512,64]{0,1:T(8,128)(2,1)S(1)}, bf16[512,64]{0,1:T(8,128)(2,1)}, u32[]{:S(2)}) copy-start(bf16[512,64]{0,1:T(8,128)(2,1)} %param.9) | copy-start | bytes 196612
  63.7 338.6 %copy-start.3 = (s32[512]{0:T(512)S(1)}, s32[512]{0:T(512)}, u32[]{:S(2)}) copy-start(s32[512]{0:T(512)} %param.7) | copy-start | bytes 6148
  344.9 48.4 %collective-permute-start = (bf16[16384,64]{0,1:T(8,128)(2,1)}, bf16[16384,64]{0,1:T(8,128)(2,1)S(1)}, u32[]{:S(2)}, u32[]{:S(2)}) collective-permute-start(bf16[16384,64]{0,1:T(8,128)(2,1)} %all-gather.2.cloned.1.call-done), channel_id=1, source_target_pairs={{0,32},{32,64},{64,96},{96,0},{1,33},{33,65},{65,97},{97,1},{2,34}... | collective-permute-start | bytes 6291464 | tf_op jit(solution)/shard_map/ppermute | solution.py:26
  346.2 97.7 %collective-permute-start.2 = (bf16[16384,64]{0,1:T(8,128)(2,1)}, bf16[16384,64]{0,1:T(8,128)(2,1)}, u32[]{:S(2)}, u32[]{:S(2)}) collective-permute-start(bf16[16384,64]{0,1:T(8,128)(2,1)} %all-gather.2.cloned.1.call-done), channel_id=1, source_target_pairs={{32,0},{64,32},{96,64},{0,96},{33,1},{65,33},{97,65},{1,97},{34,2}... | collective-permute-start | bytes 6291464 | tf_op jit(solution)/shard_map/ppermute | solution.py:29
  393.3 50.6 %collective-permute-start.1 = (bf16[16384,64]{0,1:T(8,128)(2,1)S(1)}, bf16[16384,64]{0,1:T(8,128)(2,1)}, u32[]{:S(2)}, u32[]{:S(2)}) collective-permute-start(bf16[16384,64]{0,1:T(8,128)(2,1)S(1)} %collective-permute-done), channel_id=1, source_target_pairs={{0,32},{32,64},{64,96},{96,0},{1,33},{33,65},{65,97},{97,1},{2,34}... | collective-permute-start | bytes 6291464 | tf_op jit(solution)/shard_map/ppermute | solution.py:26
  394.2 48.7 %all-to-all-start.3 = ((s32[128,4,1]{1,2,0:T(1,128)}), s32[128,4,1]{1,2,0:T(1,128)S(1)}, u32[]{:S(2)}, u32[]{:S(2)}) async-start(s32[128,4,1]{1,2,0:T(1,128)} %bitcast.13), calls=%async_computation.3 | async-start | bytes 131072 | tf_op jit(solution)/shard_map/all_to_all | solution.py:50
  554.9 23.4 %copy-start = (bf16[512,128,64]{1,2,0:T(8,128)(2,1)S(1)}, bf16[512,128,64]{1,2,0:T(8,128)(2,1)}, u32[]{:S(2)}) copy-start(bf16[512,128,64]{1,2,0:T(8,128)(2,1)} %gather_fusion.1) | copy-start | bytes 25165828
Sparse Core Ops, SparseCore 0:
  269.6 75.2 all-gather.1
